TPU v7x, 256 devices: a whole 4x4x8 slice. The times are simulated.
256 devices in a mesh: wide: 32 (over x, y, core), blk: 8 (over z).
Axes of the slice: x: 4, y: 4, z: 8, core: 2. Of those that a mesh axis runs over, the one named last changes fastest.
Arguments:
- tokens: bfloat16 [1024, 8192], P('wide', 'blk'), may hold values from -6 to 6
- target: bfloat16 [1024, 8192], P('wide', 'blk'), may hold values from -3 to 3
- probe_vector: float32 [8192], P('blk'), may hold values from -12 to 12
- weight_in: bfloat16 [256, 8, 2, 128, 128], P('wide', 'blk'), may hold values from -0.375 to 0.375
- weight_out: bfloat16 [256, 8, 2, 128, 128], P('wide', 'blk'), may hold values from -0.09375 to 0.09375
- slot_rows: int32 [256, 8, 2], P('wide', 'blk'), may hold values from 0 to 7, as said below
- slot_count: int32 [256, 8], P('wide', 'blk'), may hold values from 0 to 2, as said below
Outputs:
- outputs: bfloat16 [1024, 8192], P('wide', 'blk')
- token_grad: bfloat16 [1024, 8192], P('wide', 'blk')
- grad_in: float32 [256, 8, 2, 128, 128], P('wide', 'blk')
- grad_out: float32 [256, 8, 2, 128, 128], P('wide', 'blk')
Inputs may be any that keep to these rules, and one draw needn't show every extreme that they name: `slot_rows`: the 2 entries of one (j, g) are distinct feature blocks of the row group. `slot_count`: every hidden block column has 2 used slots in at least one row group.
All inputs are finite; a program needn't handle non-finite values.
Results may differ from a plain program's by a relative error of at most 0.033.
Values may be sent and summed in bfloat16 or wider, within the bound.
No kernel may reach another device: no remote copies, remote signals or barrier semaphores. Data moves between devices by JAX's collectives and lax.ppermute only.
A program may use at most 64 MiB of HBM per device.

v0:
```python
import math
import jax
import jax.numpy as jnp
from jax import lax
from jax.sharding import PartitionSpec as P


def activate(value):
    return jax.nn.gelu(value, approximate=True)


def activate_slope(value):
    return jax.jvp(activate, (value,), (jnp.ones_like(value),))[1]


def row_stride(count, limit):
    return math.gcd(count, limit)


def by_blocks(blockfn, row_count, limit):
    stride = row_stride(row_count, limit)
    pieces = lax.map(
        lambda index: blockfn(index * stride, stride),
        jnp.arange(row_count // stride, dtype=jnp.int32),
    )
    return pieces.reshape((row_count,) + pieces.shape[2:])


def pick_rows(activity, row_index, block):
    row_total = activity.shape[0]
    columns, slots = row_index.shape
    blocks = activity.reshape(row_total, activity.shape[1] // block, block)
    return jnp.take(blocks, row_index.reshape(-1), axis=1).reshape(row_total, columns, slots, block)


def body(tokens, target, probe_vector, weight_in, weight_out, slot_rows, slot_count):
    columns, unit, slots, block, width_two = weight_in.shape
    features = tokens.shape[1]
    feature_blocks = features // block
    row_index = slot_rows[:, 0]
    in_use = lax.broadcasted_iota(jnp.int32, (columns, slots), 1) < slot_count[:, 0][:, None]
    mask_low = in_use.astype(jnp.bfloat16)[:, :, None, None]
    mask_full = in_use.astype(jnp.float32)[:, :, None, None]
    tiles_in = weight_in[:, 0] * mask_low
    tiles_out = weight_out[:, 0] * mask_low
    onehot = (
        row_index[:, :, None]
        == lax.broadcasted_iota(jnp.int32, (columns, slots, feature_blocks), 2)
    ).astype(jnp.float32)
    chosen = jnp.take(
        probe_vector.reshape(feature_blocks, block), row_index.reshape(-1), axis=0
    ).reshape(columns, slots, block)
    image_part = jnp.einsum(
        "jsk,jskn->jn", chosen, tiles_in.astype(jnp.float32), precision=lax.Precision.HIGHEST
    )
    image, norm_probe = lax.psum((image_part, jnp.sum(probe_vector * probe_vector)), "blk")
    norm_image = lax.psum(jnp.sum(image * image), "wide")
    spectral = jnp.sqrt(norm_image / norm_probe)
    x_full = lax.all_gather(tokens, "wide", axis=0, tiled=True)
    all_rows = x_full.shape[0]
    block_rows = all_rows // lax.axis_size("blk")
    owned = tokens.shape[0]

    def hidden_block_term(start_row, count):
        picked = pick_rows(lax.dynamic_slice_in_dim(x_full, start_row, count, 0), row_index, block)
        product = jnp.einsum("tjsk,jskn->tjn", picked, tiles_in, preferred_element_type=jnp.float32)
        return product.reshape(count, columns * block)

    hidden_own = (
        lax.psum_scatter(
            by_blocks(hidden_block_term, block_rows * lax.axis_size("blk"), 512).astype(
                jnp.bfloat16
            ),
            "blk",
            scatter_dimension=0,
            tiled=True,
        ).astype(jnp.float32)
        / spectral
    )
    active_own = activate(hidden_own).astype(jnp.bfloat16)
    active_full = lax.all_gather(active_own, "blk", axis=0, tiled=True)

    def output_block_term(start_row, count):
        active = lax.dynamic_slice_in_dim(active_full, start_row, count, 0).reshape(
            count, columns, block
        )
        contrib = jnp.einsum(
            "tjk,jskn->tjsn", active, tiles_out, preferred_element_type=jnp.float32
        )
        return jnp.einsum("tjsn,jsr->trn", contrib, onehot).reshape(count, features)

    outputs = lax.psum_scatter(
        by_blocks(output_block_term, owned * lax.axis_size("wide"), 256).astype(jnp.bfloat16),
        "wide",
        scatter_dimension=0,
        tiled=True,
    )
    residual = (outputs.astype(jnp.float32) - target.astype(jnp.float32)).astype(jnp.bfloat16)
    error_full = lax.all_gather(residual, "wide", axis=0, tiled=True)

    def back_block_term(start_row, count):
        picked = pick_rows(
            lax.dynamic_slice_in_dim(error_full, start_row, count, 0), row_index, block
        )
        product = jnp.einsum(
            "tjsn,jskn->tjk", picked, tiles_out, preferred_element_type=jnp.float32
        )
        return product.reshape(count, columns * block)

    back_own = lax.psum_scatter(
        by_blocks(back_block_term, block_rows * lax.axis_size("blk"), 512).astype(jnp.bfloat16),
        "blk",
        scatter_dimension=0,
        tiled=True,
    ).astype(jnp.float32)
    slope_own = (back_own * activate_slope(hidden_own)).astype(jnp.bfloat16)
    slope_full = lax.all_gather(slope_own, "blk", axis=0, tiled=True)
    stride = row_stride(all_rows, 256)

    def grads_block(index, totals):
        start_row = index * stride
        picked_in = pick_rows(
            lax.dynamic_slice_in_dim(x_full, start_row, stride, 0), row_index, block
        )
        picked_err = pick_rows(
            lax.dynamic_slice_in_dim(error_full, start_row, stride, 0), row_index, block
        )
        slope = lax.dynamic_slice_in_dim(slope_full, start_row, stride, 0).reshape(
            stride, columns, block
        )
        active = lax.dynamic_slice_in_dim(active_full, start_row, stride, 0).reshape(
            stride, columns, block
        )
        part_in = jnp.einsum("tjsk,tjn->jskn", picked_in, slope, preferred_element_type=jnp.float32)
        part_out = jnp.einsum(
            "tjk,tjsn->jskn", active, picked_err, preferred_element_type=jnp.float32
        )
        return (totals[0] + part_in, totals[1] + part_out)

    empty = jnp.zeros((columns, slots, block, block), jnp.float32)
    raw_in, raw_out = lax.fori_loop(0, all_rows // stride, grads_block, (empty, empty))
    raw_in = raw_in * mask_full
    grad_out = raw_out * mask_full
    curvature = lax.psum(jnp.sum(raw_in * tiles_in.astype(jnp.float32)), ("wide", "blk"))
    outer = jnp.einsum("jsk,jn->jskn", chosen, image) * mask_full
    grad_in = raw_in / spectral - curvature / (spectral**3 * norm_probe) * outer

    def input_block_term(start_row, count):
        slope = lax.dynamic_slice_in_dim(slope_full, start_row, count, 0).reshape(
            count, columns, block
        )
        contrib = jnp.einsum("tjn,jskn->tjsk", slope, tiles_in, preferred_element_type=jnp.float32)
        return jnp.einsum("tjsk,jsr->trk", contrib, onehot).reshape(count, features)

    token_grad = (
        lax.psum_scatter(
            by_blocks(input_block_term, owned * lax.axis_size("wide"), 256).astype(jnp.bfloat16),
            "wide",
            scatter_dimension=0,
            tiled=True,
        ).astype(jnp.float32)
        / spectral
    ).astype(jnp.bfloat16)
    return (outputs, token_grad, grad_in[:, None], grad_out[:, None])


def solution(mesh):
    in_specs = (
        P("wide", "blk"),
        P("wide", "blk"),
        P("blk"),
        P("wide", "blk", None, None, None),
        P("wide", "blk", None, None, None),
        P("wide", "blk", None),
        P("wide", "blk"),
    )
    out_specs = (
        P("wide", "blk"),
        P("wide", "blk"),
        P("wide", "blk", None, None, None),
        P("wide", "blk", None, None, None),
    )
    return jax.shard_map(body, mesh=mesh, in_specs=in_specs, out_specs=out_specs, check_vma=False)
```

profile of v0, /device:TPU:1, one launch (start us, length us, event | category | flops | bytes accessed | tf_op | source)
XLA Modules:
  0.0 652.1 jit_solution(13190907771488800029)
XLA Ops:
  9.5 2.1 bitcast_multiply_fusion
  12.7 51.0 %all-gather.5.cloned.1.call-done = bf16[1024,1024]{1,0:T(8,128)(2,1)} async-done(((bf16[32,1024]{1,0:T(8,128)(2,1)}), bf16[1024,1024]{1,0:T(8,128)(2,1)}) %all-gather.5.cloned.1.call-update) | async-done | bytes 2097168 | tf_op jit(solution)/shard_map/all_gather | solution.py:59
  63.7 3.9 copy.95
  67.6 1.5 broadcast.110.clone
  69.1 15.2 %while.63 = (s32[]{:T(128)}, bf16[2,512,1024]{1,2,0:T(8,128)(2,1)}, s32[2]{0:T(128)S(1)}, bf16[1024,1024]{0,1:T(8,128)(2,1)}, s32[8,1,2]{2,0,1:T(8,128)}, /*inde...) while((s32[]{:T(128)}, bf16[2,512,1024]{1,2,0:T(8,128)(2,1)}, ...), condition=%wide.wide.region_1.3_spmd, body=%wide.wide.region_0.0_spmd.sunk | while | flops 269485216 | bytes 37229152 | solution.py:22
  70.3 1.3 constant_dynamic-slice_fusion.20
  75.3 1.3 copy-done.11
  77.9 1.3 constant_dynamic-slice_fusion.20
  82.9 1.3 copy-done.11
  84.3 3.9 copy.132
  90.7 15.5 %all-reduce = (f32[8,128]{1,0:T(8,128)S(1)}, f32[]{:T(128)}) all-reduce(f32[8,128]{1,0:T(8,128)S(1)} %bitcast.244, f32[]{:T(128)} %multiply_reduce_fusion.1), channel_id=1, replica_groups=mesh['wide'=32,'blk'=8] {'blk'}, use_global_device_ids=true, to_apply=%region_3.5 | all-reduce | flops 1025 | bytes 8200 | tf_op jit(solution)/shard_map/psum | solution.py:56
  106.8 65.7 %psum.29 = f32[]{:T(128)} all-reduce(f32[]{:T(128)} %multiply_reduce_fusion.2), channel_id=1, replica_groups=mesh['wide'=32,'blk'=8] {'wide'}, use_global_device_ids=true, to_apply=%region_5.7 | all-reduce | flops 1 | bytes 8 | tf_op jit(solution)/shard_map/psum | solution.py:57
  173.9 1.1 copy.129
  176.0 37.4 %all-gather.7.cloned.1.call-done = bf16[1024,1024]{0,1:T(8,128)(2,1)} async-done(((bf16[128,1024]{0,1:T(8,128)(2,1)}), bf16[1024,1024]{0,1:T(8,128)(2,1)}) %all-gather.7.cloned.1.call-update) | async-done | bytes 2097168 | tf_op jit(solution)/shard_map/all_gather | solution.py:81
  213.4 1.6 broadcast.109.clone
  215.0 18.3 %while.61 = (s32[]{:T(128)}, bf16[4,256,1024]{2,1,0:T(8,128)(2,1)}, s32[4]{0:T(128)S(1)}, bf16[1024,1024]{0,1:T(8,128)(2,1)}, bf16[8,2,128,128]{3,2,1,0:T(8,128)...) while((s32[]{:T(128)}, bf16[4,256,1024]{2,1,0:T(8,128)(2,1)}, ...), condition=%wide.region_9.11_spmd.clone, body=%wide.region_8.10_spmd.clone.sunk | while | flops 142606592 | bytes 6816483 | solution.py:22
  216.3 1.1 constant_dynamic-slice_fusion.18
  220.9 1.1 constant_dynamic-slice_fusion.18
  225.4 1.1 constant_dynamic-slice_fusion.18
  230.0 1.1 constant_dynamic-slice_fusion.18
  233.4 87.8 %reduce-scatter.9.cloned.1.call-done = bf16[32,1024]{1,0:T(8,128)(2,1)} async-done(((bf16[1024,1024]{1,0:T(8,128)(2,1)}), bf16[32,1024]{1,0:T(8,128)(2,1)}) %reduce-scatter.9.cloned.1.call-update) | async-done | bytes 65552 | tf_op jit(solution)/shard_map/reduce_scatter | solution.py:92
  321.3 1.5 subtract_convert_fusion
  322.9 51.6 %all-gather.9.cloned.1.call-done = bf16[1024,1024]{1,0:T(8,128)(2,1)} async-done(((bf16[32,1024]{1,0:T(8,128)(2,1)}), bf16[1024,1024]{1,0:T(8,128)(2,1)}) %all-gather.9.cloned.1.call-update) | async-done | bytes 2097168 | tf_op jit(solution)/shard_map/all_gather | solution.py:99
  374.5 3.9 copy.101
  378.5 1.5 broadcast.110
  380.0 15.5 %while.64 = (s32[]{:T(128)}, bf16[2,512,1024]{1,2,0:T(8,128)(2,1)}, s32[2]{0:T(128)S(1)}, bf16[1024,1024]{0,1:T(8,128)(2,1)}, s32[8,1,2]{2,0,1:T(8,128)}, /*inde...) while((s32[]{:T(128)}, bf16[2,512,1024]{1,2,0:T(8,128)(2,1)}, ...), condition=%wide.wide.region_12.14_spmd, body=%wide.wide.region_11.13_spmd.sunk | while | flops 269485216 | bytes 39326336 | solution.py:22
  381.3 1.3 constant_dynamic-slice_fusion.21
  386.4 1.4 copy-done.13
  389.1 1.3 constant_dynamic-slice_fusion.21
  394.1 1.4 copy-done.13
  395.5 4.0 copy.133
  399.5 37.0 %reduce-scatter.15.cloned.1.call-done = bf16[128,1024]{1,0:T(8,128)(2,1)} async-done(((bf16[1024,1024]{1,0:T(8,128)(2,1)}), bf16[128,1024]{1,0:T(8,128)(2,1)}) %reduce-scatter.15.cloned.1.call-update) | async-done | bytes 262160
  436.6 1.1 copy.131
  437.7 1.1 fusion.32
  439.1 46.3 %all-gather.11.cloned.1.call-done = bf16[1024,1024]{0,1:T(8,128)(2,1)} async-done(((bf16[128,1024]{0,1:T(8,128)(2,1)}), bf16[1024,1024]{0,1:T(8,128)(2,1)}) %all-gather.11.cloned.1.call-update) | async-done | bytes 2097168 | tf_op jit(solution)/shard_map/all_gather | solution.py:117
  485.5 1.7 broadcast.109
  487.1 18.8 %while.62 = (s32[]{:T(128)}, bf16[4,256,1024]{2,1,0:T(8,128)(2,1)}, s32[4]{0:T(128)S(1)}, bf16[1024,1024]{0,1:T(8,128)(2,1)}, bf16[8,2,128,128]{3,2,1,0:T(8,128)...) while((s32[]{:T(128)}, bf16[4,256,1024]{2,1,0:T(8,128)(2,1)}, ...), condition=%wide.region_15.17_spmd.clone, body=%wide.region_14.16_spmd.clone.sunk | while | flops 142606592 | bytes 6816483 | solution.py:22
  488.5 1.1 constant_dynamic-slice_fusion.19
  493.2 1.1 constant_dynamic-slice_fusion.19
  505.9 51.6 %while.65 = (s32[]{:T(128)}, f32[8,2,128,128]{3,2,1,0:T(8,128)}, f32[8,2,128,128]{2,3,1,0:T(8,128)}, bf16[1024,1024]{0,1:T(8,128)(2,1)}, s32[8,1,2]{2,0,1:T(8,12...) while((s32[]{:T(128)}, f32[8,2,128,128]{3,2,1,0:T(8,128)}, ...), condition=%wide.wide.region_18.21_spmd.clone, body=%wide.wide.region_17.20_spmd.clone.sunk | while | flops 270533760 | bytes 28316308 | solution.py:141
  506.0 2.1 constant_dynamic-slice_fusion.22
  509.1 2.1 constant_dynamic-slice_fusion.23
  512.3 1.2 broadcast_select_fusion.13
  513.5 2.6 fusion.105
  516.2 1.5 convolution_add_fusion.3
  517.6 2.1 constant_dynamic-slice_fusion.22
  520.8 2.1 constant_dynamic-slice_fusion.23
  524.0 1.2 broadcast_select_fusion.13
  525.2 3.0 fusion.105
  528.2 2.7 convolution_add_fusion.3
  530.9 2.1 constant_dynamic-slice_fusion.22
  534.1 2.1 constant_dynamic-slice_fusion.23
  537.3 1.2 broadcast_select_fusion.13
  538.5 3.0 fusion.105
  541.5 2.7 convolution_add_fusion.3
  544.2 2.1 constant_dynamic-slice_fusion.22
  547.4 2.1 constant_dynamic-slice_fusion.23
  550.6 1.2 broadcast_select_fusion.13
  551.8 3.0 fusion.105
  554.8 2.7 convolution_add_fusion.3
  557.5 2.4 multiply_reduce_fusion
  560.5 79.3 %psum.31 = f32[]{:T(128)} all-reduce(f32[]{:T(128)} %multiply_reduce_fusion), channel_id=1, replica_groups=mesh['wide'=32,'blk'=8] {'wide','blk'}, use_global_device_ids=true, to_apply=%region_20.23 | all-reduce | flops 1 | bytes 8 | tf_op jit(solution)/shard_map/psum | solution.py:144
  640.8 2.9 multiply_bitcast_fusion
  643.7 1.5 divide_convert_fusion
  (210 shorter events, 58.6 us)
Async XLA Ops:
  7.2 56.5 %all-gather.5.cloned.1.call-start = ((), (), s32[]{:S(2)}) async-start(), calls=%async_computation.4 | async-start | bytes 2162688 | tf_op jit(solution)/shard_map/all_gather | solution.py:59
  7.9 165.9 %reduce-scatter.13.cloned.1.call-start = ((), (), s32[]{:S(2)}) async-start(), calls=%async_computation.10 | async-start | bytes 2359296
  8.7 58.9 %copy-start.16 = (s32[8,1,2]{2,0,1:T(8,128)}, s32[8,1,2]{2,0,1:T(8,128)S(1)}, u32[]{:S(2)}) copy-start(s32[8,1,2]{2,0,1:T(8,128)S(1)} %copy.96) | copy-start | bytes 196
  11.6 57.5 %copy-start.5 = (bf16[8,2,128,128]{3,2,1,0:T(8,128)(2,1)}, bf16[8,2,128,128]{3,2,1,0:T(8,128)(2,1)S(1)}, u32[]{:S(2)}) copy-start(bf16[8,2,128,128]{3,2,1,0:T(8,128)(2,1)S(1)} %get-tuple-element.952) | copy-start | bytes 1572868
  73.3 1.0 copy-start.9
  73.6 1.6 copy-start.10
  75.3 1.4 copy-start.11
  80.9 1.0 copy-start.9
  81.2 1.6 copy-start.10
  82.9 1.4 copy-start.11
  88.2 0.7 copy-start.17
  88.2 0.8 copy-start.15
  88.2 0.9 copy-start.14
  88.2 2.1 copy-start.6
  88.3 126.8 %copy-start.1 = (bf16[8,2,128,128]{3,2,1,0:T(8,128)(2,1)S(1)}, bf16[8,2,128,128]{3,2,1,0:T(8,128)(2,1)}, u32[]{:S(2)}) copy-start(bf16[8,2,128,128]{3,2,1,0:T(8,128)(2,1)} %get-tuple-element.920) | copy-start | bytes 1572868
  88.3 125.1 %all-gather.7.cloned.1.call-start = ((), (), s32[]{:S(2)}) async-start(), calls=%async_computation.5 | async-start | bytes 2359296 | tf_op jit(solution)/shard_map/all_gather | solution.py:81
  175.9 145.3 %reduce-scatter.9.cloned.1.call-start = ((), (), s32[]{:S(2)}) async-start(), calls=%async_computation.6 | async-start | bytes 2162688 | tf_op jit(solution)/shard_map/reduce_scatter | solution.py:92
  233.3 87.9 %copy-start.19 = (bf16[32,1024]{1,0:T(8,128)(2,1)S(1)}, bf16[32,1024]{1,0:T(8,128)(2,1)}, u32[]{:S(2)}) copy-start(bf16[32,1024]{1,0:T(8,128)(2,1)} %param.22) | copy-start | bytes 196612
  233.4 141.2 %all-gather.9.cloned.1.call-start = ((), (), s32[]{:S(2)}) async-start(), calls=%async_computation.7 | async-start | bytes 2162688 | tf_op jit(solution)/shard_map/all_gather | solution.py:99
  322.8 113.8 %reduce-scatter.15.cloned.1.call-start = ((), (), s32[]{:S(2)}) async-start(), calls=%async_computation.11 | async-start | bytes 2359296
  380.0 2.6 copy-start.2
  384.3 1.0 copy-start.3
  384.6 1.6 copy-start.12
  386.3 1.4 copy-start.13
  387.7 2.6 copy-start.2
  392.0 1.0 copy-start.3
  392.3 1.6 copy-start.12
  394.1 1.4 copy-start.13
  399.5 39.6 %copy-start.18 = (s32[8,1,2]{2,0,1:T(8,128)S(1)}, s32[8,1,2]{2,0,1:T(8,128)}, u32[]{:S(2)}) copy-start(s32[8,1,2]{2,0,1:T(8,128)} %get-tuple-element.1050) | copy-start | bytes 196
  399.5 87.6 %copy-start.7 = (bf16[8,2,128,128]{3,2,1,0:T(8,128)(2,1)S(1)}, bf16[8,2,128,128]{3,2,1,0:T(8,128)(2,1)}, u32[]{:S(2)}) copy-start(bf16[8,2,128,128]{3,2,1,0:T(8,128)(2,1)} %copy-done.5) | copy-start | bytes 1572868
  399.5 86.0 %all-gather.11.cloned.1.call-start = ((), (), s32[]{:S(2)}) async-start(), calls=%async_computation.8 | async-start | bytes 2359296 | tf_op jit(solution)/shard_map/all_gather | solution.py:117
  438.8 204.9 %reduce-scatter.11.cloned.1.call-start = ((), (), s32[]{:S(2)}) async-start(), calls=%async_computation.9 | async-start | bytes 2162688 | tf_op jit(solution)/shard_map/reduce_scatter | solution.py:156
  513.5 2.6 copy-start
  513.5 2.6 copy-start.4
  525.2 3.0 copy-start
  525.2 3.0 copy-start.4
  538.5 3.0 copy-start
  538.5 3.0 copy-start.4
  551.8 3.0 copy-start
  551.8 3.0 copy-start.4
  557.5 82.3 %copy-start.8 = (f32[8,2,128,128]{2,3,1,0:T(8,128)S(1)}, f32[8,2,128,128]{2,3,1,0:T(8,128)}, u32[]{:S(2)}) copy-start(f32[8,2,128,128]{2,3,1,0:T(8,128)} %get-tuple-element.279) | copy-start | bytes 3145732
Sparse Core Ops, SparseCore 0:
  10.6 53.0 all-gather.4
  88.4 37.0 reduce-scatter.12
  176.0 37.3 all-gather.6
  233.5 87.7 reduce-scatter.8
  324.2 50.2 all-gather.8
  399.6 36.9 reduce-scatter.14
  438.9 46.4 all-gather.10
  506.1 87.7 reduce-scatter.10
where the time goes:
time: 654 us; the launch traced here: 652 us
  waiting for transfers between devices  312 us (48%)
  blocking collectives  161 us (25%)
  local copies, waits for them, and re-layouts  98.7 us (15%)
  matrix products  34 us (5%)
  other arithmetic  20.6 us (3%)
  between operations  16.8 us (3%)
  loops' own time  8.79 us (1%)
    reduce_scatter x1, waiting for transfers between devices, body(): lax.psum_scatter(by_blocks(output_block_term, owned * lax.axis_size('wide...  87.8 us
    psum x1, blocking collectives, body(): lax.psum(jnp.sum(raw_in * tiles_in.astype(jnp.float32)), ('wide', 'blk'))  79.3 us
    psum x1, blocking collectives, body(): norm_image = lax.psum(jnp.sum(image * image), 'wide')  65.7 us
    all_gather x1, waiting for transfers between devices, body(): error_full = lax.all_gather(residual, 'wide', axis=0, tiled=True)  51.6 us
    all_gather x1, waiting for transfers between devices, body(): x_full = lax.all_gather(tokens, 'wide', axis=0, tiled=True)  51 us
    all_gather x1, waiting for transfers between devices, body(): slope_full = lax.all_gather(slope_own, 'blk', axis=0, tiled=True)  46.3 us
    unnamed x10, waiting for transfers between devices  37.8 us
    all_gather x1, waiting for transfers between devices, body(): active_full = lax.all_gather(active_own, 'blk', axis=0, tiled=True)  37.4 us
  transfers between devices with their start and end apart: 8, of which 6 were waited for; matrix products, arithmetic and copies ran while one was open for 10% of the time, Pallas kernels for 0%

commit v1 on v0

--- a/solution.py
+++ b/solution.py
@@ -114,7 +114,15 @@
         tiled=True,
     ).astype(jnp.float32)
     slope_own = (back_own * activate_slope(hidden_own)).astype(jnp.bfloat16)
-    slope_full = lax.all_gather(slope_own, "blk", axis=0, tiled=True)
+    q_n = lax.axis_size("blk")
+    copies = [(q, (q + 1) % q_n) for q in range(q_n)]
+    taken_in = [None] * q_n
+    taken_in[q_n - 1] = slope_own
+    for j in range(q_n - 2, -1, -1):
+        taken_in[j] = lax.ppermute(taken_in[j + 1], "blk", copies)
+    seen_now = jnp.concatenate(taken_in, 0)
+    known = (lax.axis_index("blk") + 1) * slope_own.shape[0]
+    slope_full = jnp.roll(seen_now, shift=known, axis=0)
     stride = row_stride(all_rows, 256)
 
     def grads_block(index, totals):

time: 654 us -> 668 us (1.021)
  waiting for transfers between devices: 312 us -> 319 us
    ppermute x0 -> x7, waiting for transfers between devices: none -> 53 us  [body(): taken_in[j] = lax.ppermute(taken_in[j + 1], 'blk', copies)]
    all_gather x1 -> x0, waiting for transfers between devices: 46.3 us -> none  [body(): slope_full = lax.all_gather(slope_own, 'blk', axis=0, tiled=True)]
    unnamed x10 -> x9, waiting for transfers between devices: 37.8 us -> 37.8 us
  transfers between devices with their start and end apart: 8 -> 14, of which waited for: 6 -> 12; matrix products, arithmetic and copies ran while one was open for 10% -> 10% of each run, Pallas kernels for 0% -> 0%
where the time goes in v1:
time: 668 us; the launch traced here: 667 us
  waiting for transfers between devices  319 us (48%)
  blocking collectives  167 us (25%)
  local copies, waits for them, and re-layouts  101 us (15%)
  matrix products  34 us (5%)
  other arithmetic  19.9 us (3%)
  between operations  16.8 us (3%)
  loops' own time  8.34 us (1%)
    reduce_scatter x1, waiting for transfers between devices, body(): lax.psum_scatter(by_blocks(output_block_term, owned * lax.axis_size('wide...  87.8 us
    psum x1, blocking collectives, body(): lax.psum(jnp.sum(raw_in * tiles_in.astype(jnp.float32)), ('wide', 'blk'))  85.6 us
    psum x1, blocking collectives, body(): norm_image = lax.psum(jnp.sum(image * image), 'wide')  65.7 us
    ppermute x7, waiting for transfers between devices, body(): taken_in[j] = lax.ppermute(taken_in[j + 1], 'blk', copies)  53 us
    all_gather x1, waiting for transfers between devices, body(): error_full = lax.all_gather(residual, 'wide', axis=0, tiled=True)  51.7 us
    all_gather x1, waiting for transfers between devices, body(): x_full = lax.all_gather(tokens, 'wide', axis=0, tiled=True)  51 us
    unnamed x9, waiting for transfers between devices  37.8 us
    all_gather x1, waiting for transfers between devices, body(): active_full = lax.all_gather(active_own, 'blk', axis=0, tiled=True)  37.5 us
  transfers between devices with their start and end apart: 14, of which 12 were waited for; matrix products, arithmetic and copies ran while one was open for 10% of the time, Pallas kernels for 0%

profile of v1, /device:TPU:1, one launch (start us, length us, event | category | flops | bytes accessed | tf_op | source)
XLA Modules:
  0.0 666.5 jit_solution(8611630969942310779)
XLA Ops:
  9.5 2.1 bitcast_multiply_fusion
  12.7 51.0 %all-gather.4.cloned.1.call-done = bf16[1024,1024]{1,0:T(8,128)(2,1)} async-done(((bf16[32,1024]{1,0:T(8,128)(2,1)}), bf16[1024,1024]{1,0:T(8,128)(2,1)}) %all-gather.4.cloned.1.call-update) | async-done | bytes 2097168 | tf_op jit(solution)/shard_map/all_gather | solution.py:59
  63.7 3.9 copy.95
  67.6 1.5 broadcast.111.clone
  69.1 15.2 %while.63 = (s32[]{:T(128)}, bf16[2,512,1024]{1,2,0:T(8,128)(2,1)}, s32[2]{0:T(128)S(1)}, bf16[1024,1024]{0,1:T(8,128)(2,1)}, s32[8,1,2]{2,0,1:T(8,128)}, /*inde...) while((s32[]{:T(128)}, bf16[2,512,1024]{1,2,0:T(8,128)(2,1)}, ...), condition=%wide.wide.region_1.3_spmd, body=%wide.wide.region_0.0_spmd.sunk | while | flops 269485216 | bytes 37229152 | solution.py:22
  70.3 1.3 constant_dynamic-slice_fusion.21
  75.3 1.3 copy-done.11
  77.9 1.3 constant_dynamic-slice_fusion.21
  82.9 1.3 copy-done.11
  84.3 3.9 copy.132
  90.7 15.5 %all-reduce = (f32[8,128]{1,0:T(8,128)S(1)}, f32[]{:T(128)}) all-reduce(f32[8,128]{1,0:T(8,128)S(1)} %bitcast.244, f32[]{:T(128)} %multiply_reduce_fusion.1), channel_id=1, replica_groups=mesh['wide'=32,'blk'=8] {'blk'}, use_global_device_ids=true, to_apply=%region_3.5 | all-reduce | flops 1025 | bytes 8200 | tf_op jit(solution)/shard_map/psum | solution.py:56
  106.8 65.7 %psum.29 = f32[]{:T(128)} all-reduce(f32[]{:T(128)} %multiply_reduce_fusion.2), channel_id=1, replica_groups=mesh['wide'=32,'blk'=8] {'wide'}, use_global_device_ids=true, to_apply=%region_5.7 | all-reduce | flops 1 | bytes 8 | tf_op jit(solution)/shard_map/psum | solution.py:57
  173.8 1.1 copy.129
  175.9 37.5 %all-gather.6.cloned.1.call-done = bf16[1024,1024]{0,1:T(8,128)(2,1)} async-done(((bf16[128,1024]{0,1:T(8,128)(2,1)}), bf16[1024,1024]{0,1:T(8,128)(2,1)}) %all-gather.6.cloned.1.call-update) | async-done | bytes 2097168 | tf_op jit(solution)/shard_map/all_gather | solution.py:81
  213.4 1.6 broadcast.110.clone
  215.0 18.3 %while.61 = (s32[]{:T(128)}, bf16[4,256,1024]{2,1,0:T(8,128)(2,1)}, s32[4]{0:T(128)S(1)}, bf16[1024,1024]{0,1:T(8,128)(2,1)}, bf16[8,2,128,128]{3,2,1,0:T(8,128)...) while((s32[]{:T(128)}, bf16[4,256,1024]{2,1,0:T(8,128)(2,1)}, ...), condition=%wide.region_9.11_spmd.clone, body=%wide.region_8.10_spmd.clone.sunk | while | flops 142606592 | bytes 6816483 | solution.py:22
  233.4 87.8 %reduce-scatter.9.cloned.1.call-done = bf16[32,1024]{1,0:T(8,128)(2,1)} async-done(((bf16[1024,1024]{1,0:T(8,128)(2,1)}), bf16[32,1024]{1,0:T(8,128)(2,1)}) %reduce-scatter.9.cloned.1.call-update) | async-done | bytes 65552 | tf_op jit(solution)/shard_map/reduce_scatter | solution.py:92
  321.2 1.5 subtract_convert_fusion
  322.8 51.7 %all-gather.8.cloned.1.call-done = bf16[1024,1024]{1,0:T(8,128)(2,1)} async-done(((bf16[32,1024]{1,0:T(8,128)(2,1)}), bf16[1024,1024]{1,0:T(8,128)(2,1)}) %all-gather.8.cloned.1.call-update) | async-done | bytes 2097168 | tf_op jit(solution)/shard_map/all_gather | solution.py:99
  374.5 3.9 copy.101
  378.5 1.5 broadcast.111
  380.0 15.4 %while.64 = (s32[]{:T(128)}, bf16[2,512,1024]{1,2,0:T(8,128)(2,1)}, s32[2]{0:T(128)S(1)}, bf16[1024,1024]{0,1:T(8,128)(2,1)}, s32[8,1,2]{2,0,1:T(8,128)}, /*inde...) while((s32[]{:T(128)}, bf16[2,512,1024]{1,2,0:T(8,128)(2,1)}, ...), condition=%wide.wide.region_12.14_spmd, body=%wide.wide.region_11.13_spmd.sunk | while | flops 269485216 | bytes 39326336 | solution.py:22
  381.3 1.3 constant_dynamic-slice_fusion.22
  386.3 1.4 copy-done.13
  389.0 1.3 constant_dynamic-slice_fusion.22
  394.0 1.4 copy-done.13
  395.4 4.0 copy.133
  399.4 37.0 %reduce-scatter.15.cloned.1.call-done = bf16[128,1024]{1,0:T(8,128)(2,1)} async-done(((bf16[1024,1024]{1,0:T(8,128)(2,1)}), bf16[128,1024]{1,0:T(8,128)(2,1)}) %reduce-scatter.15.cloned.1.call-update) | async-done | bytes 262160
  436.5 1.1 copy.131
  438.1 6.4 collective-permute-done
  444.5 7.9 %collective-permute-done.1 = bf16[128,1024]{0,1:T(8,128)(2,1)S(1)} collective-permute-done((bf16[128,1024]{0,1:T(8,128)(2,1)S(1)}, bf16[128,1024]{0,1:T(8,128)(2,1)S(1)}, u32[]{:S(2)}, u32[]{:S(2)}) %collective-permute-start.1) | collective-permute-done | bytes 262176 | tf_op jit(solution)/shard_map/ppermute | solution.py:122
  452.4 9.0 %collective-permute-done.2 = bf16[128,1024]{0,1:T(8,128)(2,1)S(1)} collective-permute-done((bf16[128,1024]{0,1:T(8,128)(2,1)S(1)}, bf16[128,1024]{0,1:T(8,128)(2,1)S(1)}, u32[]{:S(2)}, u32[]{:S(2)}) %collective-permute-start.2) | collective-permute-done | bytes 262176 | tf_op jit(solution)/shard_map/ppermute | solution.py:122
  461.4 8.7 %collective-permute-done.3 = bf16[128,1024]{0,1:T(8,128)(2,1)S(1)} collective-permute-done((bf16[128,1024]{0,1:T(8,128)(2,1)S(1)}, bf16[128,1024]{0,1:T(8,128)(2,1)S(1)}, u32[]{:S(2)}, u32[]{:S(2)}) %collective-permute-start.3) | collective-permute-done | bytes 262176 | tf_op jit(solution)/shard_map/ppermute | solution.py:122
  470.1 7.8 %collective-permute-done.4 = bf16[128,1024]{0,1:T(8,128)(2,1)S(1)} collective-permute-done((bf16[128,1024]{0,1:T(8,128)(2,1)S(1)}, bf16[128,1024]{0,1:T(8,128)(2,1)S(1)}, u32[]{:S(2)}, u32[]{:S(2)}) %collective-permute-start.4) | collective-permute-done | bytes 262176 | tf_op jit(solution)/shard_map/ppermute | solution.py:122
  477.9 6.9 %collective-permute-done.5 = bf16[128,1024]{0,1:T(8,128)(2,1)S(1)} collective-permute-done((bf16[128,1024]{0,1:T(8,128)(2,1)S(1)}, bf16[128,1024]{0,1:T(8,128)(2,1)S(1)}, u32[]{:S(2)}, u32[]{:S(2)}) %collective-permute-start.5) | collective-permute-done | bytes 262176 | tf_op jit(solution)/shard_map/ppermute | solution.py:122
  484.8 6.3 collective-permute-done.6
  492.6 1.6 constant_dynamic-slice_fusion.8
  494.3 1.6 broadcast.110
  495.9 18.0 %while.62 = (s32[]{:T(128)}, bf16[4,256,1024]{2,1,0:T(8,128)(2,1)}, s32[4]{0:T(128)S(1)}, bf16[1024,1024]{0,1:T(8,128)(2,1)}, bf16[8,2,128,128]{3,2,1,0:T(8,128)...) while((s32[]{:T(128)}, bf16[4,256,1024]{2,1,0:T(8,128)(2,1)}, ...), condition=%wide.region_15.17_spmd.clone, body=%wide.region_14.16_spmd.clone.sunk | while | flops 142606592 | bytes 6816483 | solution.py:22
  514.0 51.7 %while.65 = (s32[]{:T(128)}, f32[8,2,128,128]{3,2,1,0:T(8,128)}, f32[8,2,128,128]{2,3,1,0:T(8,128)}, bf16[1024,1024]{0,1:T(8,128)(2,1)}, s32[8,1,2]{2,0,1:T(8,12...) while((s32[]{:T(128)}, f32[8,2,128,128]{3,2,1,0:T(8,128)}, ...), condition=%wide.wide.region_18.21_spmd.clone, body=%wide.wide.region_17.20_spmd.clone.sunk | while | flops 270533760 | bytes 28316308 | solution.py:149
  514.0 2.1 constant_dynamic-slice_fusion.23
  517.2 2.1 constant_dynamic-slice_fusion.24
  520.4 1.2 broadcast_select_fusion.13
  521.6 2.6 fusion.105
  524.2 1.5 convolution_add_fusion.3
  525.7 2.1 constant_dynamic-slice_fusion.23
  528.9 2.1 constant_dynamic-slice_fusion.24
  532.1 1.2 broadcast_select_fusion.13
  533.3 3.0 fusion.105
  536.3 2.7 convolution_add_fusion.3
  539.0 2.2 constant_dynamic-slice_fusion.23
  542.2 2.1 constant_dynamic-slice_fusion.24
  545.4 1.2 broadcast_select_fusion.13
  546.6 3.0 fusion.105
  549.6 2.7 convolution_add_fusion.3
  552.3 2.2 constant_dynamic-slice_fusion.23
  555.6 2.1 constant_dynamic-slice_fusion.24
  558.7 1.2 broadcast_select_fusion.13
  560.0 3.0 fusion.105
  563.0 2.7 convolution_add_fusion.3
  565.7 2.4 multiply_reduce_fusion
  568.6 85.6 %psum.31 = f32[]{:T(128)} all-reduce(f32[]{:T(128)} %multiply_reduce_fusion), channel_id=1, replica_groups=mesh['wide'=32,'blk'=8] {'wide','blk'}, use_global_device_ids=true, to_apply=%region_20.23 | all-reduce | flops 1 | bytes 8 | tf_op jit(solution)/shard_map/psum | solution.py:152
  655.3 2.9 multiply_bitcast_fusion
  658.2 1.5 divide_convert_fusion
  (238 shorter events, 66.4 us)
Async XLA Ops:
  7.2 56.5 %all-gather.4.cloned.1.call-start = ((), (), s32[]{:S(2)}) async-start(), calls=%async_computation.4 | async-start | bytes 2162688 | tf_op jit(solution)/shard_map/all_gather | solution.py:59
  7.9 165.9 %reduce-scatter.13.cloned.1.call-start = ((), (), s32[]{:S(2)}) async-start(), calls=%async_computation.9 | async-start | bytes 2359296
  8.7 58.9 %copy-start.16 = (s32[8,1,2]{2,0,1:T(8,128)}, s32[8,1,2]{2,0,1:T(8,128)S(1)}, u32[]{:S(2)}) copy-start(s32[8,1,2]{2,0,1:T(8,128)S(1)} %copy.96) | copy-start | bytes 196
  11.6 57.5 %copy-start.5 = (bf16[8,2,128,128]{3,2,1,0:T(8,128)(2,1)}, bf16[8,2,128,128]{3,2,1,0:T(8,128)(2,1)S(1)}, u32[]{:S(2)}) copy-start(bf16[8,2,128,128]{3,2,1,0:T(8,128)(2,1)S(1)} %get-tuple-element.952) | copy-start | bytes 1572868
  73.3 1.0 copy-start.9
  73.6 1.6 copy-start.10
  75.3 1.4 copy-start.11
  80.9 1.0 copy-start.9
  81.2 1.6 copy-start.10
  82.9 1.4 copy-start.11
  88.2 0.7 copy-start.17
  88.2 0.8 copy-start.15
  88.2 0.9 copy-start.14
  88.2 2.1 copy-start.6
  88.2 126.7 %copy-start.1 = (bf16[8,2,128,128]{3,2,1,0:T(8,128)(2,1)S(1)}, bf16[8,2,128,128]{3,2,1,0:T(8,128)(2,1)}, u32[]{:S(2)}) copy-start(bf16[8,2,128,128]{3,2,1,0:T(8,128)(2,1)} %get-tuple-element.920) | copy-start | bytes 1572868
  88.3 125.1 %all-gather.6.cloned.1.call-start = ((), (), s32[]{:S(2)}) async-start(), calls=%async_computation.5 | async-start | bytes 2359296 | tf_op jit(solution)/shard_map/all_gather | solution.py:81
  175.9 145.3 %reduce-scatter.9.cloned.1.call-start = ((), (), s32[]{:S(2)}) async-start(), calls=%async_computation.6 | async-start | bytes 2162688 | tf_op jit(solution)/shard_map/reduce_scatter | solution.py:92
  233.3 87.9 %copy-start.19 = (bf16[32,1024]{1,0:T(8,128)(2,1)S(1)}, bf16[32,1024]{1,0:T(8,128)(2,1)}, u32[]{:S(2)}) copy-start(bf16[32,1024]{1,0:T(8,128)(2,1)} %param.22) | copy-start | bytes 196612
  233.3 141.2 %all-gather.8.cloned.1.call-start = ((), (), s32[]{:S(2)}) async-start(), calls=%async_computation.7 | async-start | bytes 2162688 | tf_op jit(solution)/shard_map/all_gather | solution.py:99
  322.7 113.8 %reduce-scatter.15.cloned.1.call-start = ((), (), s32[]{:S(2)}) async-start(), calls=%async_computation.10 | async-start | bytes 2359296
  380.0 2.6 copy-start.2
  384.3 1.0 copy-start.3
  384.6 1.6 copy-start.12
  386.3 1.4 copy-start.13
  387.7 2.6 copy-start.2
  392.0 1.0 copy-start.3
  392.3 1.6 copy-start.12
  394.0 1.4 copy-start.13
  399.4 85.4 %copy-start.18 = (s32[8,1,2]{2,0,1:T(8,128)S(1)}, s32[8,1,2]{2,0,1:T(8,128)}, u32[]{:S(2)}) copy-start(s32[8,1,2]{2,0,1:T(8,128)} %get-tuple-element.1060) | copy-start | bytes 196
  399.4 258.8 %reduce-scatter.11.cloned.1.call-start = ((), (), s32[]{:S(2)}) async-start(), calls=%async_computation.8 | async-start | bytes 2162688 | tf_op jit(solution)/shard_map/reduce_scatter | solution.py:164
  438.0 6.5 collective-permute-start
  444.5 7.9 %collective-permute-start.1 = (bf16[128,1024]{0,1:T(8,128)(2,1)S(1)}, bf16[128,1024]{0,1:T(8,128)(2,1)S(1)}, u32[]{:S(2)}, u32[]{:S(2)}) collective-permute-start(bf16[128,1024]{0,1:T(8,128)(2,1)S(1)} %collective-permute-done), channel_id=1, source_target_pairs={{0,1},{1,2},{2,3},{3,4},{4,5},{5,6},{6,7},{7,0},{8,9},{9,10},{10,1... | collective-permute-start | bytes 786440 | tf_op jit(solution)/shard_map/ppermute | solution.py:122
  452.4 9.0 %collective-permute-start.2 = (bf16[128,1024]{0,1:T(8,128)(2,1)S(1)}, bf16[128,1024]{0,1:T(8,128)(2,1)S(1)}, u32[]{:S(2)}, u32[]{:S(2)}) collective-permute-start(bf16[128,1024]{0,1:T(8,128)(2,1)S(1)} %collective-permute-done.1), channel_id=1, source_target_pairs={{0,1},{1,2},{2,3},{3,4},{4,5},{5,6},{6,7},{7,0},{8,9},{9,10},{10,1... | collective-permute-start | bytes 786440 | tf_op jit(solution)/shard_map/ppermute | solution.py:122
  461.4 8.7 %collective-permute-start.3 = (bf16[128,1024]{0,1:T(8,128)(2,1)S(1)}, bf16[128,1024]{0,1:T(8,128)(2,1)S(1)}, u32[]{:S(2)}, u32[]{:S(2)}) collective-permute-start(bf16[128,1024]{0,1:T(8,128)(2,1)S(1)} %collective-permute-done.2), channel_id=1, source_target_pairs={{0,1},{1,2},{2,3},{3,4},{4,5},{5,6},{6,7},{7,0},{8,9},{9,10},{10,1... | collective-permute-start | bytes 786440 | tf_op jit(solution)/shard_map/ppermute | solution.py:122
  470.1 7.8 %collective-permute-start.4 = (bf16[128,1024]{0,1:T(8,128)(2,1)S(1)}, bf16[128,1024]{0,1:T(8,128)(2,1)S(1)}, u32[]{:S(2)}, u32[]{:S(2)}) collective-permute-start(bf16[128,1024]{0,1:T(8,128)(2,1)S(1)} %collective-permute-done.3), channel_id=1, source_target_pairs={{0,1},{1,2},{2,3},{3,4},{4,5},{5,6},{6,7},{7,0},{8,9},{9,10},{10,1... | collective-permute-start | bytes 786440 | tf_op jit(solution)/shard_map/ppermute | solution.py:122
  477.9 6.9 %collective-permute-start.5 = (bf16[128,1024]{0,1:T(8,128)(2,1)S(1)}, bf16[128,1024]{0,1:T(8,128)(2,1)S(1)}, u32[]{:S(2)}, u32[]{:S(2)}) collective-permute-start(bf16[128,1024]{0,1:T(8,128)(2,1)S(1)} %collective-permute-done.4), channel_id=1, source_target_pairs={{0,1},{1,2},{2,3},{3,4},{4,5},{5,6},{6,7},{7,0},{8,9},{9,10},{10,1... | collective-permute-start | bytes 786440 | tf_op jit(solution)/shard_map/ppermute | solution.py:122
  484.7 6.4 collective-permute-start.6
  494.3 1.6 copy-start.7
  521.6 2.6 copy-start
  521.6 2.6 copy-start.4
  533.3 3.0 copy-start
  533.3 3.0 copy-start.4
  546.6 3.0 copy-start
  546.6 3.0 copy-start.4
  560.0 3.0 copy-start
  560.0 3.0 copy-start.4
  565.7 88.6 %copy-start.8 = (f32[8,2,128,128]{2,3,1,0:T(8,128)S(1)}, f32[8,2,128,128]{2,3,1,0:T(8,128)}, u32[]{:S(2)}) copy-start(f32[8,2,128,128]{2,3,1,0:T(8,128)} %get-tuple-element.279) | copy-start | bytes 3145732
Sparse Core Ops, SparseCore 0:
  10.6 53.0 all-gather.3
  88.4 37.1 reduce-scatter.12
  176.0 37.3 all-gather.5
  233.4 87.6 reduce-scatter.8
  324.1 50.3 all-gather.7
  399.5 36.9 reduce-scatter.14
  514.1 94.8 reduce-scatter.10
